TPU v7x, 256 devices: a whole 4x4x8 slice. The times are simulated.
256 devices in a mesh: dp: 4 (over x), node: 2 (over core), local: 32 (over z, y).
Axes of the slice: x: 4, y: 4, z: 8, core: 2. Of those that a mesh axis runs over, the one named last changes fastest.
Arguments:
- tokens: bfloat16 [32768, 2048], P(('dp', 'node', 'local')), may hold values from -6 to 6
- cotangent: bfloat16 [32768, 2048], P(('dp', 'node', 'local')), may hold values from -4 to 4
- routes: int32 [32768, 8], P(('dp', 'node', 'local')), may hold values from 0 to 63, all different within a row; in each aligned block of 128 rows (0 to 127, 128 to 255, ...) at most 24 rows name the same one
- gates: bfloat16 [32768, 8], P(('dp', 'node', 'local')), may hold values from 0.029907227 to 0.3984375
- w_gate: bfloat16 [64, 2048, 384], P(('node', 'local'), 'dp'), may hold values from -0.125 to 0.125
- w_up: bfloat16 [64, 2048, 384], P(('node', 'local'), 'dp'), may hold values from -0.125 to 0.125
- w_down: bfloat16 [64, 2048, 384], P(('node', 'local'), 'dp'), may hold values from -0.3125 to 0.3125
Outputs:
- input_grad: bfloat16 [32768, 2048], P(('dp', 'node', 'local'))
- gate_grad: bfloat16 [32768, 8], P(('dp', 'node', 'local'))
- gate_weight_grad: float32 [64, 2048, 384], P(('node', 'local'), 'dp')
- up_weight_grad: float32 [64, 2048, 384], P(('node', 'local'), 'dp')
- down_weight_grad: float32 [64, 2048, 384], P(('node', 'local'), 'dp')
Inputs may be any that keep to these rules, and one draw needn't show every extreme that they name: `routes`: each token names 8 different experts. Among the tokens of one device no expert is named more than 24 times, and on some device some expert is named exactly 24 times.
All inputs are finite; a program needn't handle non-finite values.
Results may differ from a plain program's by a relative error of at most 0.0057.
Values may be sent and summed in bfloat16 or wider, within the bound.
No kernel may reach another device: no remote copies, remote signals or barrier semaphores. Data moves between devices by JAX's collectives and lax.ppermute only.
A program may use at most 128 MiB of HBM per device.

v0:
```python
import jax
import jax.numpy as jnp
from jax import lax
from jax.sharding import PartitionSpec as P


def expert_rows(rows_x, rows_dy, rows_gate, gate_proj, up_proj, down_proj):
    pre_gate = jnp.dot(rows_x, gate_proj, preferred_element_type=jnp.float32)
    pre_up = jnp.dot(rows_x, up_proj, preferred_element_type=jnp.float32)
    gate_sigmoid = jax.nn.sigmoid(pre_gate)
    activated = pre_gate * gate_sigmoid
    hidden = activated * pre_up
    upstream = jnp.dot(rows_dy, down_proj, preferred_element_type=jnp.float32)
    gate_grad = jnp.sum(upstream * hidden, axis=1).astype(jnp.bfloat16)
    weight = rows_gate.astype(jnp.float32)[:, None]
    scaled_hidden = (weight * hidden).astype(jnp.bfloat16)
    hidden_grad = weight * upstream
    pre_gate_grad = (
        hidden_grad * pre_up * gate_sigmoid * (1.0 + pre_gate * (1.0 - gate_sigmoid))
    ).astype(jnp.bfloat16)
    pre_up_grad = (hidden_grad * activated).astype(jnp.bfloat16)
    over_rows = (((0,), (0,)), ((), ()))
    down_grad = lax.dot_general(
        rows_dy, scaled_hidden, over_rows, preferred_element_type=jnp.float32
    )
    gate_wgrad = lax.dot_general(
        rows_x, pre_gate_grad, over_rows, preferred_element_type=jnp.float32
    )
    up_wgrad = lax.dot_general(rows_x, pre_up_grad, over_rows, preferred_element_type=jnp.float32)
    over_hidden = (((1,), (1,)), ((), ()))
    input_rows = lax.dot_general(
        pre_gate_grad, gate_proj, over_hidden, preferred_element_type=jnp.float32
    )
    input_rows = input_rows + lax.dot_general(
        pre_up_grad, up_proj, over_hidden, preferred_element_type=jnp.float32
    )
    return (input_rows.astype(jnp.bfloat16), gate_grad, gate_wgrad, up_wgrad, down_grad)


def local(tokens, cotangent, routes, gates, w_gate, w_up, w_down):
    tokens_dev, top_count = routes.shape
    width = tokens.shape[1]
    hidden_units = w_gate.shape[2]
    cores = lax.axis_size("node")
    planes = lax.axis_size("lz")
    rows_of = lax.axis_size("ly")
    experts = cores * planes * rows_of
    capacity = min(
        tokens_dev,
        max(3 * tokens_dev * top_count // (2 * experts), tokens_dev * top_count // experts),
    )
    near = cores * rows_of
    slots = near * planes * capacity
    half = width // 2
    meta = jnp.concatenate([gates, routes.astype(jnp.bfloat16)], axis=1).reshape(1, -1)
    meta = jnp.pad(meta, ((0, 0), (0, width - meta.shape[1])))
    seen_row = lax.all_gather(meta, "lz", axis=0, tiled=False)
    seen_x = lax.all_gather(tokens, "lz", axis=0, tiled=False)
    seen_dy = lax.all_gather(cotangent, "lz", axis=0, tiled=False)
    seen_meta = seen_row[:, 0, : 2 * tokens_dev * top_count].reshape(
        planes, tokens_dev, 2 * top_count
    )
    seen_gates = seen_meta[..., :top_count]
    seen_routes = seen_meta[..., top_count:].astype(jnp.int32)
    plane = lax.axis_index("lz")
    near_ids = jnp.arange(near, dtype=jnp.int32)
    near_experts = near_ids // rows_of * (planes * rows_of) + plane * rows_of + near_ids % rows_of
    hit = seen_routes[..., None] == near_experts
    named = jnp.any(hit, axis=2)
    earlier = (jnp.arange(tokens_dev)[:, None] > jnp.arange(tokens_dev)[None, :]).astype(
        jnp.bfloat16
    )
    rank = jnp.einsum(
        "ts,zsj->jzt", earlier, named.astype(jnp.bfloat16), preferred_element_type=jnp.float32
    ).astype(jnp.int32)
    choose = jnp.transpose(named, (2, 0, 1))[:, :, None, :] & (
        rank[:, :, None, :] == jnp.arange(capacity, dtype=jnp.int32)[None, None, :, None]
    )
    choose_b = choose.astype(jnp.bfloat16)
    gate_tj = jnp.sum(jnp.where(hit, seen_gates[..., None], jnp.zeros((), jnp.bfloat16)), axis=2)
    send_gate = jnp.sum(
        jnp.where(
            choose, jnp.transpose(gate_tj, (2, 0, 1))[:, :, None, :], jnp.zeros((), jnp.bfloat16)
        ),
        axis=3,
    )
    gate_row = jnp.pad(
        send_gate.reshape(near, 1, planes * capacity),
        ((0, 0), (0, 0), (0, width - planes * capacity)),
    )
    send_x = jnp.einsum(
        "jzrt,ztd->jzrd", choose_b, seen_x, preferred_element_type=jnp.float32
    ).astype(jnp.bfloat16)
    send_x = jnp.concatenate([send_x.reshape(near, planes * capacity, width), gate_row], axis=1)
    send_dy = (
        jnp.einsum("jzrt,ztd->jzrd", choose_b, seen_dy, preferred_element_type=jnp.float32)
        .astype(jnp.bfloat16)
        .reshape(near, planes * capacity, width)
    )
    all_weights = lax.all_gather(
        jnp.concatenate([w_gate, w_up, w_down], axis=2), "dp", axis=1, tiled=True
    )[0]
    gate_proj = all_weights[:, :hidden_units]
    up_proj = all_weights[:, hidden_units : 2 * hidden_units]
    down_proj = all_weights[:, 2 * hidden_units :]
    recv_x = lax.all_to_all(send_x, ("node", "ly"), split_axis=0, concat_axis=0, tiled=True)
    recv_dy = lax.all_to_all(send_dy, ("node", "ly"), split_axis=0, concat_axis=0, tiled=True)
    results = expert_rows(
        recv_x[:, : planes * capacity, :].reshape(slots, width),
        recv_dy.reshape(slots, width),
        recv_x[:, planes * capacity, : planes * capacity].reshape(slots),
        gate_proj,
        up_proj,
        down_proj,
    )
    grad_row = jnp.pad(
        results[1].reshape(near, 1, planes * capacity),
        ((0, 0), (0, 0), (0, half - planes * capacity)),
    )
    back_lo = jnp.concatenate(
        [results[0][:, :half].reshape(near, planes * capacity, half), grad_row], axis=1
    )
    back_hi = results[0][:, half:].reshape(near, planes * capacity, width - half)
    home_lo = lax.all_to_all(back_lo, ("node", "ly"), split_axis=0, concat_axis=0, tiled=True)
    home_gate = home_lo[:, planes * capacity, : planes * capacity].reshape(near, planes, capacity)
    home_lo = home_lo[:, : planes * capacity, :].reshape(near, planes, capacity, half)
    home_hi = lax.all_to_all(
        back_hi, ("node", "ly"), split_axis=0, concat_axis=0, tiled=True
    ).reshape(near, planes, capacity, width - half)
    partial_lo = jnp.einsum("jzrt,jzrd->ztd", choose_b, home_lo, preferred_element_type=jnp.float32)
    gate_jzt = jnp.sum(jnp.where(choose, home_gate[..., None], jnp.zeros((), jnp.bfloat16)), axis=2)
    pick_gate = jnp.sum(
        jnp.where(
            hit, jnp.transpose(gate_jzt, (1, 2, 0))[:, :, None, :], jnp.zeros((), jnp.bfloat16)
        ),
        axis=3,
    )
    gate_cols = jnp.pad(
        pick_gate.astype(jnp.float32).reshape(planes, 1, tokens_dev * top_count),
        ((0, 0), (0, 0), (0, half - tokens_dev * top_count)),
    )
    summed_down = lax.psum_scatter(results[4], "dp", scatter_dimension=0, tiled=True)
    summed = lax.psum_scatter(
        jnp.concatenate([results[2], results[3]], axis=1), "dp", scatter_dimension=0, tiled=True
    )
    summed_down, summed, partial_lo, gate_cols = lax.optimization_barrier(
        (summed_down, summed, partial_lo, gate_cols)
    )
    reduced_lo = lax.psum_scatter(
        jnp.concatenate([partial_lo, gate_cols], axis=1), "lz", scatter_dimension=0, tiled=True
    )[0]
    partial_hi = jnp.einsum("jzrt,jzrd->ztd", choose_b, home_hi, preferred_element_type=jnp.float32)
    reduced_hi = lax.psum_scatter(partial_hi, "lz", scatter_dimension=0, tiled=True)[0]
    input_grad = jnp.concatenate([reduced_lo[:tokens_dev], reduced_hi], axis=1).astype(jnp.bfloat16)
    gate_grad = (
        reduced_lo[tokens_dev, : tokens_dev * top_count]
        .reshape(tokens_dev, top_count)
        .astype(jnp.bfloat16)
    )
    return (
        input_grad,
        gate_grad,
        summed[None, :, :hidden_units],
        summed[None, :, hidden_units : 2 * hidden_units],
        summed_down[None],
    )


def solution(mesh):
    local_size = mesh.shape["local"]
    rows_of = 4 if local_size % 4 == 0 else 1
    split = jax.sharding.Mesh(
        mesh.devices.reshape(mesh.shape["dp"], mesh.shape["node"], local_size // rows_of, rows_of),
        ("dp", "node", "lz", "ly"),
    )
    rows = P(("dp", "node", "lz", "ly"), None)
    expert = P(("node", "lz", "ly"), "dp", None)
    return jax.shard_map(
        local,
        mesh=split,
        in_specs=(rows, rows, rows, rows, expert, expert, expert),
        out_specs=(rows, rows, expert, expert, expert),
        check_vma=False,
    )
```

profile of v0, /device:TPU:1, one launch (start us, length us, event | category | flops | bytes accessed | tf_op | source)
XLA Modules:
  0.0 475.3 jit_solution(9930952564812045546)
XLA Ops:
  10.3 23.4 %all_gather.22 = bf16[8,1,2048]{2,1,0:T(2,128)(2,1)S(1)} all-gather(bf16[1,1,2048]{2,1,0:T(2,128)(2,1)S(1)} %all_gather.21), channel_id=1, replica_groups=mesh['dp'=4,'node'=2,'lz'=8,'ly'=4] {'lz'}, dimensions={0}, use_global_device_ids=true | all-gather | bytes 36864 | tf_op jit(solution)/shard_map/all_gather | solution.py:57
  35.3 33.4 %all-gather.10.cloned.1.call-done = bf16[1024,2048]{1,0:T(8,128)(2,1)} async-done(((bf16[128,2048]{1,0:T(8,128)(2,1)}), bf16[1024,2048]{1,0:T(8,128)(2,1)}) %all-gather.10.cloned.1.call-update) | async-done | bytes 4194320 | tf_op jit(solution)/shard_map/all_gather | solution.py:58
  68.7 4.0 convert_bitcast_fusion
  77.1 5.5 %all-to-all-start.1 = ((bf16[8,193,2048]{2,1,0:T(8,128)(2,1)}), bf16[8,193,2048]{2,1,0:T(8,128)(2,1)}, u32[]{:S(2)}, u32[]{:S(2)}) async-start(bf16[8,193,2048]{2,1,0:T(8,128)(2,1)} %fusion.1), calls=%async_computation.1 | async-start | bytes 13107200 | tf_op jit(solution)/shard_map/all_to_all | solution.py:106
  83.8 40.2 %all-gather.8.cloned.1.call-done = bf16[1024,2048]{1,0:T(8,128)(2,1)} async-done(((bf16[128,2048]{1,0:T(8,128)(2,1)}), bf16[1024,2048]{1,0:T(8,128)(2,1)}) %all-gather.8.cloned.1.call-update) | async-done | bytes 4194320 | tf_op jit(solution)/shard_map/all_gather | solution.py:59
  123.9 4.0 convert_bitcast_fusion.1
  131.1 25.9 %all-to-all-done.1 = bf16[8,193,2048]{2,1,0:T(8,128)(2,1)} async-done(((bf16[8,193,2048]{2,1,0:T(8,128)(2,1)}), bf16[8,193,2048]{2,1,0:T(8,128)(2,1)}, u32[]{:S(2)}, u32[]{:S(2)}) %all-to-all-start.1) | async-done | bytes 6324256 | tf_op jit(solution)/shard_map/all_to_all | solution.py:106
  157.0 4.8 %all-to-all-start = ((bf16[8,192,2048]{2,1,0:T(8,128)(2,1)}), bf16[8,192,2048]{2,1,0:T(8,128)(2,1)}, u32[]{:S(2)}, u32[]{:S(2)}) async-start(bf16[8,192,2048]{2,1,0:T(8,128)(2,1)} %bitcast.59), calls=%async_computation | async-start | bytes 12582912 | tf_op jit(solution)/shard_map/all_to_all | solution.py:107
  162.8 6.6 %slice.70 = bf16[8,192,2048]{2,1,0:T(8,128)(2,1)} slice(bf16[8,193,2048]{2,1,0:T(8,128)(2,1)} %all-to-all-done.1), slice={[0:8], [0:192], [0:2048]} | slice | bytes 12582912 | tf_op jit(solution)/shard_map/slice | solution.py:109
  169.4 10.1 %all-gather.6.cloned.1.call-done = bf16[1,2048,1152]{2,1,0:T(8,128)(2,1)} async-done(((bf16[1,512,1152]{2,1,0:T(8,128)(2,1)}), bf16[1,2048,1152]{2,1,0:T(8,128)(2,1)}) %all-gather.6.cloned.1.call-update) | async-done | bytes 4718608 | tf_op jit(solution)/shard_map/all_gather | solution.py:100
  179.6 7.4 %fusion.18 = f32[1536,384]{0,1:T(8,128)} fusion(bf16[1536,2048]{1,0:T(8,128)(2,1)} %bitcast.67, bf16[2048,1152]{1,0:T(8,128)(2,1)} %bitcast.71), kind=kOutput, calls=%fused_computation.26 | convolution fusion | flops 2415919104 | bytes 10223616 | tf_op jit(solution)/shard_map/dot_general | solution.py:9
  187.0 5.5 %fusion.22 = f32[1536,384]{0,1:T(8,128)} fusion(bf16[1536,2048]{1,0:T(8,128)(2,1)S(1)} %bitcast.70, bf16[2048,1152]{1,0:T(8,128)(2,1)} %bitcast.72), kind=kOutput, calls=%fused_computation.30 | convolution fusion | flops 2415919104 | bytes 10223616 | tf_op jit(solution)/shard_map/dot_general | solution.py:8
  192.5 40.5 %all-to-all-done = bf16[8,192,2048]{2,1,0:T(8,128)(2,1)} async-done(((bf16[8,192,2048]{2,1,0:T(8,128)(2,1)}), bf16[8,192,2048]{2,1,0:T(8,128)(2,1)}, u32[]{:S(2)}, u32[]{:S(2)}) %all-to-all-start) | async-done | bytes 6291488 | tf_op jit(solution)/shard_map/all_to_all | solution.py:107
  233.0 9.4 %fusion.24 = f32[2048,384]{1,0:T(8,128)} fusion(bf16[1536,2048]{1,0:T(8,128)(2,1)} %bitcast.8, f32[1536]{0:T(1024)S(1)} %reshape.115, f32[1536,384]{0,1:T(8,128)} %fusion.18, f32[1536,384]{0,1:T(8,128)} %fusion.22), kind=kOutput, calls=%fused_computation.32 | convolution fusion | flops 2420047872 | bytes 14161920 | tf_op jit(solution)/shard_map/dot_general | solution.py:23
  242.8 8.4 %multiply_reduce_fusion = (bf16[1536]{0:T(1024)(128)(2,1)S(1)}, bf16[1536,384]{0,1:T(8,128)(2,1)S(1)}, bf16[1536,384]{0,1:T(8,128)(2,1)S(1)}) fusion(f32[1536,384]{0,1:T(8,128)} %fusion.18, f32[1536,384]{0,1:T(8,128)} %fusion.22, f32[1536]{0:T(1024)S(1)} %reshape.115, bf16[1536,2048]{1,0:T(8,128)(2,1)} %bitcast.8, bf16[2048,1152]{1,0:T(8,128)(2,1)} %bitcast.73), kind=kOutput, calls=%fused_computation.15 | convolution fusion | flops 2425944576 | bytes 14951424 | tf_op jit(solution)/shard_map/dot_general | solution.py:13
  251.2 5.2 %fusion.56 = f32[2048,384]{0,1:T(8,128)S(1)} fusion(bf16[1536,384]{0,1:T(8,128)(2,1)S(1)} %get-tuple-element.39, bf16[1536,2048]{1,0:T(8,128)(2,1)} %bitcast.68), kind=kOutput, calls=%fused_computation.79 | convolution fusion | flops 2415919104 | bytes 10616832 | tf_op jit(solution)/shard_map/dot_general | solution.py:26
  256.3 4.8 %fusion.57 = f32[2048,384]{0,1:T(8,128)S(1)} fusion(bf16[1536,384]{0,1:T(8,128)(2,1)S(1)} %get-tuple-element.42, bf16[1536,2048]{1,0:T(8,128)(2,1)} %bitcast.69), kind=kOutput, calls=%fused_computation.80 | convolution fusion | flops 2415919104 | bytes 10616832 | tf_op jit(solution)/shard_map/dot_general | solution.py:29
  264.5 4.9 %fusion.20 = f32[1536,2048]{1,0:T(8,128)S(1)} fusion(bf16[1536,384]{0,1:T(8,128)(2,1)S(1)} %get-tuple-element.39, bf16[2048,1152]{1,0:T(8,128)(2,1)} %bitcast.74), kind=kOutput, calls=%fused_computation.28 | convolution fusion | flops 2415919104 | bytes 15335424 | tf_op jit(solution)/shard_map/dot_general | solution.py:31
  269.4 5.5 %add_convert_fusion = bf16[1536,2048]{1,0:T(8,128)(2,1)S(1)} fusion(f32[1536,2048]{1,0:T(8,128)S(1)} %fusion.20, bf16[1536,384]{0,1:T(8,128)(2,1)} %copy-done.3, bf16[2048,1152]{1,0:T(8,128)(2,1)} %bitcast.75), kind=kOutput, calls=%fused_computation.2 | convolution fusion | flops 2422210560 | bytes 21626880 | tf_op jit(solution)/shard_map/dot_general | solution.py:34
  277.3 41.4 %all_to_all.20 = bf16[8,192,1024]{2,1,0:T(8,128)(2,1)S(1)} all-to-all(bf16[8,192,1024]{2,1,0:T(8,128)(2,1)S(1)} %bitcast.64), channel_id=1, replica_groups=mesh['dp'=4,'node'=2,'lz'=8,'ly'=4] {'node','ly'}, dimensions={0} | all-to-all | bytes 6291456 | tf_op jit(solution)/shard_map/all_to_all | solution.py:127
  323.8 41.8 %all_to_all.21 = bf16[8,193,1024]{2,1,0:T(8,128)(2,1)S(1)} all-to-all(bf16[8,193,1024]{2,1,0:T(8,128)(2,1)S(1)} %fusion.3), channel_id=1, replica_groups=mesh['dp'=4,'node'=2,'lz'=8,'ly'=4] {'node','ly'}, dimensions={0} | all-to-all | bytes 6324224 | tf_op jit(solution)/shard_map/all_to_all | solution.py:124
  371.7 4.9 %pad_maximum_fusion.1 = f32[8,129,1024]{2,1,0:T(8,128)} fusion(f32[8,1,1024]{2,1,0:T(1,128)S(1)} %copy.69, f32[8,128,1024]{2,1,0:T(8,128)} %fusion.9), kind=kLoop, calls=%fused_computation.9 | loop fusion | flops 1056768 | bytes 8454144 | tf_op jit(solution)/shard_map/concatenate | solution.py:150
  376.7 30.0 %reduce-scatter.11.cloned.1.call-done = f32[1,128,1024]{2,1,0:T(8,128)} async-done(((f32[8,128,1024]{2,1,0:T(8,128)}), f32[1,128,1024]{2,1,0:T(8,128)}) %reduce-scatter.11.cloned.1.call-update) | async-done | bytes 524304 | tf_op jit(solution)/shard_map/reduce_scatter | solution.py:153
  410.2 55.5 %reduce-scatter.9.cloned.1.call-done = f32[1,129,1024]{2,1,0:T(8,128)} async-done(((f32[8,129,1024]{2,1,0:T(8,128)}), f32[1,129,1024]{2,1,0:T(8,128)}) %reduce-scatter.9.cloned.1.call-update) | async-done | bytes 528400 | tf_op jit(solution)/shard_map/reduce_scatter | solution.py:149
  (78 shorter events, 38.0 us)
Async XLA Ops:
  7.2 61.5 %all-gather.10.cloned.1.call-start = ((), (), s32[]{:S(2)}) async-start(), calls=%async_computation.14 | async-start | bytes 4718592 | tf_op jit(solution)/shard_map/all_gather | solution.py:58
  7.9 116.0 %all-gather.8.cloned.1.call-start = ((), (), s32[]{:S(2)}) async-start(), calls=%async_computation.13 | async-start | bytes 4718592 | tf_op jit(solution)/shard_map/all_gather | solution.py:59
  77.1 5.5 %copy-start.4 = (bf16[1,512,384]{2,1,0:T(8,128)(2,1)S(1)}, bf16[1,512,384]{2,1,0:T(8,128)(2,1)}, u32[]{:S(2)}) copy-start(bf16[1,512,384]{2,1,0:T(8,128)(2,1)} %param.13) | copy-start | bytes 1179652
  77.1 5.5 %copy-start.5 = (bf16[1,512,384]{2,1,0:T(8,128)(2,1)S(1)}, bf16[1,512,384]{2,1,0:T(8,128)(2,1)}, u32[]{:S(2)}) copy-start(bf16[1,512,384]{2,1,0:T(8,128)(2,1)} %param.12) | copy-start | bytes 1179652
  77.1 5.5 %copy-start.6 = (bf16[1,512,384]{2,1,0:T(8,128)(2,1)S(1)}, bf16[1,512,384]{2,1,0:T(8,128)(2,1)}, u32[]{:S(2)}) copy-start(bf16[1,512,384]{2,1,0:T(8,128)(2,1)} %param.11) | copy-start | bytes 1179652
  77.1 79.8 %all-to-all-start.1 = ((bf16[8,193,2048]{2,1,0:T(8,128)(2,1)}), bf16[8,193,2048]{2,1,0:T(8,128)(2,1)}, u32[]{:S(2)}, u32[]{:S(2)}) async-start(bf16[8,193,2048]{2,1,0:T(8,128)(2,1)} %fusion.1), calls=%async_computation.1 | async-start | bytes 13107200 | tf_op jit(solution)/shard_map/all_to_all | solution.py:106
  82.6 96.9 %all-gather.6.cloned.1.call-start = ((), (), s32[]{:S(2)}) async-start(), calls=%async_computation.8 | async-start | bytes 5898240 | tf_op jit(solution)/shard_map/all_gather | solution.py:100
  157.0 76.1 %all-to-all-start = ((bf16[8,192,2048]{2,1,0:T(8,128)(2,1)}), bf16[8,192,2048]{2,1,0:T(8,128)(2,1)}, u32[]{:S(2)}, u32[]{:S(2)}) async-start(bf16[8,192,2048]{2,1,0:T(8,128)(2,1)} %bitcast.59), calls=%async_computation | async-start | bytes 12582912 | tf_op jit(solution)/shard_map/all_to_all | solution.py:107
  161.8 209.9 %reduce-scatter.5.cloned.1.call-start = ((), (), s32[]{:S(2)}) async-start(), calls=%async_computation.9 | async-start | bytes 3932160 | tf_op jit(solution)/shard_map/reduce_scatter | solution.py:142
  179.5 7.4 %copy-start.1 = (bf16[8,192,2048]{2,1,0:T(8,128)(2,1)S(1)}, bf16[8,192,2048]{2,1,0:T(8,128)(2,1)}, u32[]{:S(2)}) copy-start(bf16[8,192,2048]{2,1,0:T(8,128)(2,1)} %slice.70) | copy-start | bytes 18874372
  242.5 129.2 %reduce-scatter.7.cloned.1.call-start = ((), (), s32[]{:S(2)}) async-start(), calls=%async_computation.10 | async-start | bytes 7864320 | tf_op jit(solution)/shard_map/reduce_scatter | solution.py:143
  251.1 5.2 %copy-start.3 = (bf16[1536,384]{0,1:T(8,128)(2,1)}, bf16[1536,384]{0,1:T(8,128)(2,1)S(1)}, u32[]{:S(2)}) copy-start(bf16[1536,384]{0,1:T(8,128)(2,1)S(1)} %get-tuple-element.42) | copy-start | bytes 3538948
  264.2 142.5 %reduce-scatter.11.cloned.1.call-start = ((), (), s32[]{:S(2)}) async-start(), calls=%async_computation.12 | async-start | bytes 4718592 | tf_op jit(solution)/shard_map/reduce_scatter | solution.py:153
  321.5 1.9 copy-start
  321.5 144.2 %reduce-scatter.9.cloned.1.call-start = ((), (), s32[]{:S(2)}) async-start(), calls=%async_computation.11 | async-start | bytes 5013504 | tf_op jit(solution)/shard_map/reduce_scatter | solution.py:149
  376.7 31.1 %copy-start.2 = (f32[512,768]{0,1:T(8,128)S(1)}, f32[512,768]{0,1:T(8,128)}, u32[]{:S(2)}) copy-start(f32[512,768]{0,1:T(8,128)} %reduce-scatter.7.cloned.1.call-done) | copy-start | bytes 4718596
Sparse Core Ops, SparseCore 0:
  9.8 58.8 all-gather.9
  70.5 53.4 all-gather.7
  125.8 53.7 all-gather.5
  242.6 37.8 reduce-scatter.4
  282.9 66.2 reduce-scatter.6
  351.6 55.0 reduce-scatter.10
  409.2 56.4 reduce-scatter.8
where the time goes:
time: 476 us; the launch traced here: 475 us
  waiting for transfers between devices  237 us (50%)
  blocking collectives  107 us (22%)
  matrix products  64.7 us (14%)
  local copies, waits for them, and re-layouts  22.2 us (5%)
  other arithmetic  19.3 us (4%)
  between operations  14.4 us (3%)
  starting transfers between devices  11.1 us (2%)
    reduce_scatter x1, waiting for transfers between devices, local(): lax.psum_scatter(jnp.concatenate([partial_lo, gate_cols], axis=1), 'lz',...  55.5 us
    all_to_all x1, blocking collectives, local(): lax.all_to_all(back_lo, ('node', 'ly'), split_axis=0, concat_axis=0, tile...  41.8 us
    all_to_all x1, blocking collectives, local(): lax.all_to_all(back_hi, ('node', 'ly'), split_axis=0, concat_axis=0, tile...  41.4 us
    all_to_all x1, waiting for transfers between devices, local(): lax.all_to_all(send_dy, ('node', 'ly'), split_axis=0, concat_axis=0, tile...  40.5 us
    all_gather x1, waiting for transfers between devices, local(): seen_dy = lax.all_gather(cotangent, 'lz', axis=0, tiled=False)  40.2 us
    all_gather x1, waiting for transfers between devices, local(): seen_x = lax.all_gather(tokens, 'lz', axis=0, tiled=False)  33.4 us
    reduce_scatter x1, waiting for transfers between devices, local(): lax.psum_scatter(partial_hi, 'lz', scatter_dimension=0, tiled=True)[0]  30 us
    all_to_all x1, waiting for transfers between devices, local(): lax.all_to_all(send_x, ('node', 'ly'), split_axis=0, concat_axis=0, tiled...  25.9 us
  transfers between devices with their start and end apart: 9, of which 7 were waited for; matrix products, arithmetic and copies ran while one was open for 19% of the time, Pallas kernels for 0%

commit v1 on v0

--- a/solution.py
+++ b/solution.py
@@ -2,6 +2,13 @@
 import jax.numpy as jnp
 from jax import lax
 from jax.sharding import PartitionSpec as P
+
+
+def post_orders(load, mesh_ax, k_dim):
+    shares = lax.axis_size(mesh_ax)
+    grid = tuple((shares if nth == k_dim else 1 for nth in range(load.ndim)))
+    moved = jnp.tile(load, grid)
+    return lax.all_to_all(moved, axis_name=mesh_ax, split_axis=k_dim, concat_axis=k_dim, tiled=True)
 
 
 def expert_rows(rows_x, rows_dy, rows_gate, gate_proj, up_proj, down_proj):
@@ -97,9 +104,7 @@
         .astype(jnp.bfloat16)
         .reshape(near, planes * capacity, width)
     )
-    all_weights = lax.all_gather(
-        jnp.concatenate([w_gate, w_up, w_down], axis=2), "dp", axis=1, tiled=True
-    )[0]
+    all_weights = post_orders(jnp.concatenate([w_gate, w_up, w_down], axis=2), "dp", k_dim=1)[0]
     gate_proj = all_weights[:, :hidden_units]
     up_proj = all_weights[:, hidden_units : 2 * hidden_units]
     down_proj = all_weights[:, 2 * hidden_units :]

time: 476 us -> 677 us (1.42); the launches traced: 475 us -> 667 us
  local copies, waits for them, and re-layouts: 22.2 us -> 130 us
  other arithmetic: 19.3 us -> 120 us
  waiting for transfers between devices: 237 us -> 215 us
  starting transfers between devices: 11.1 us -> 19.7 us
    unnamed x0 -> x1, other arithmetic: none -> 102 us
    another operation x0 -> x2, local copies, waits for them, and re-layouts: none -> 89 us  [post_orders(): moved = jnp.tile(load, grid)]
    all_to_all x1, waiting for transfers between devices: 25.9 us -> 65.6 us  [local(): lax.all_to_all(send_x, ('node', 'ly'), split_axis=0, concat_axis=0, tiled...]
    all_gather x1, waiting for transfers between devices: 40.2 us -> 1.22 us  [local(): seen_dy = lax.all_gather(cotangent, 'lz', axis=0, tiled=False)]
    all_gather x1, waiting for transfers between devices: 33.4 us -> 0.02 us  [local(): seen_x = lax.all_gather(tokens, 'lz', axis=0, tiled=False)]
    unnamed x18 -> x22, local copies, waits for them, and re-layouts: 4.83 us -> 26.2 us
    all_to_all x0 -> x1, waiting for transfers between devices: none -> 15.9 us  [post_orders(): lax.all_to_all(moved, axis_name=mesh_ax, split_axis=k_dim, concat_axis=k_...]
    all_gather x1 -> x0, waiting for transfers between devices: 10.1 us -> none  [local(): lax.all_gather(jnp.concatenate([w_gate, w_up, w_down], axis=2), 'dp', axi...]
  transfers between devices with their start and end apart: 9 -> 9, of which waited for: 7 -> 6; matrix products, arithmetic and copies ran while one was open for 19% -> 44% of each run, Pallas kernels for 0% -> 0%
where the time goes in v1:
time: 677 us; the launch traced here: 667 us
  waiting for transfers between devices  215 us (32%)
  local copies, waits for them, and re-layouts  130 us (19%)
  other arithmetic  120 us (18%)
  blocking collectives  108 us (16%)
  matrix products  60.1 us (9%)
  starting transfers between devices  19.7 us (3%)
  between operations  14.6 us (2%)
    unnamed x1, other arithmetic  102 us
    another operation x2, local copies, waits for them, and re-layouts, post_orders(): moved = jnp.tile(load, grid)  89 us
    all_to_all x1, waiting for transfers between devices, local(): lax.all_to_all(send_x, ('node', 'ly'), split_axis=0, concat_axis=0, tiled...  65.6 us
    reduce_scatter x1, waiting for transfers between devices, local(): lax.psum_scatter(jnp.concatenate([partial_lo, gate_cols], axis=1), 'lz',...  55.4 us
    all_to_all x1, waiting for transfers between devices, local(): lax.all_to_all(send_dy, ('node', 'ly'), split_axis=0, concat_axis=0, tile...  43 us
    all_to_all x1, blocking collectives, local(): lax.all_to_all(back_lo, ('node', 'ly'), split_axis=0, concat_axis=0, tile...  41.8 us
    all_to_all x1, blocking collectives, local(): lax.all_to_all(back_hi, ('node', 'ly'), split_axis=0, concat_axis=0, tile...  40.9 us
    reduce_scatter x1, waiting for transfers between devices, local(): lax.psum_scatter(partial_hi, 'lz', scatter_dimension=0, tiled=True)[0]  32.6 us
  transfers between devices with their start and end apart: 9, of which 6 were waited for; matrix products, arithmetic and copies ran while one was open for 44% of the time, Pallas kernels for 0%

profile of v1, /device:TPU:1, one launch (start us, length us, event | category | flops | bytes accessed | tf_op | source)
XLA Modules:
  0.0 667.2 jit_solution(5116067263723619479)
XLA Ops:
  9.6 88.7 %copy.109 = bf16[1,2048,1152]{2,0,1:T(2,128)(2,1)} copy(bf16[1,2048,1152]{2,1,0:T(8,128)(2,1)S(1)} %bitcast.72) | data formatting | bytes 9437184 | tf_op jit(solution)/shard_map/tile | solution.py:10
  98.8 101.9 %reduce.11 = bf16[2048,1152]{1,0:T(8,128)(2,1)} reduce(bf16[2048,1,1152]{2,1,0:T(2,128)(2,1)} %bitcast.68, bf16[]{:T(256)} %broadcast.105), dimensions={1}, to_apply=%bitcast.67.reduce_sub_computation | reduce | bytes 9437186
  200.7 5.5 reshape.135
  206.2 5.1 all-to-all-start.2
  212.3 25.4 %all_gather.19 = bf16[8,1,2048]{2,1,0:T(2,128)(2,1)S(1)} all-gather(bf16[1,1,2048]{2,1,0:T(2,128)(2,1)S(1)} %all_gather.18), channel_id=1, replica_groups=mesh['dp'=4,'node'=2,'lz'=8,'ly'=4] {'lz'}, dimensions={0}, use_global_device_ids=true | all-gather | bytes 36864 | tf_op jit(solution)/shard_map/all_gather | solution.py:64
  247.8 15.9 %all-to-all-done.2 = bf16[4,2,294912]{2,1,0:T(2,128)(2,1)} async-done(((bf16[4,2,294912]{2,1,0:T(2,128)(2,1)}), bf16[4,2,294912]{2,1,0:T(2,128)(2,1)}, u32[]{:S(2)}, u32[]{:S(2)}) %all-to-all-start.2) | async-done | bytes 4718624 | tf_op jit(solution)/shard_map/all_to_all | solution.py:11
  263.7 8.3 %all-to-all-start.1 = ((bf16[8,193,2048]{2,1,0:T(8,128)(2,1)}), bf16[8,193,2048]{2,1,0:T(8,128)(2,1)}, u32[]{:S(2)}, u32[]{:S(2)}) async-start(bf16[8,193,2048]{2,1,0:T(8,128)(2,1)} %fusion.1), calls=%async_computation.1 | async-start | bytes 13107200 | tf_op jit(solution)/shard_map/all_to_all | solution.py:111
  280.5 65.6 %all-to-all-done.1 = bf16[8,193,2048]{2,1,0:T(8,128)(2,1)} async-done(((bf16[8,193,2048]{2,1,0:T(8,128)(2,1)}), bf16[8,193,2048]{2,1,0:T(8,128)(2,1)}, u32[]{:S(2)}, u32[]{:S(2)}) %all-to-all-start.1) | async-done | bytes 6324256 | tf_op jit(solution)/shard_map/all_to_all | solution.py:111
  346.1 5.0 all-to-all-start
  351.4 8.1 %reshape.136 = bf16[2048,1,1152]{2,1,0:T(2,128)(2,1)} reshape(bf16[4,2,294912]{2,1,0:T(2,128)(2,1)} %all-to-all-done.2) | data formatting | bytes 9437184
  359.5 6.6 copy.108
  375.2 4.2 fusion.22
  379.4 43.0 %all-to-all-done = bf16[8,192,2048]{2,1,0:T(8,128)(2,1)} async-done(((bf16[8,192,2048]{2,1,0:T(8,128)(2,1)}), bf16[8,192,2048]{2,1,0:T(8,128)(2,1)}, u32[]{:S(2)}, u32[]{:S(2)}) %all-to-all-start) | async-done | bytes 6291488 | tf_op jit(solution)/shard_map/all_to_all | solution.py:112
  422.4 9.4 %fusion.24 = f32[2048,384]{1,0:T(8,128)} fusion(bf16[1536,2048]{1,0:T(8,128)(2,1)} %bitcast.8, f32[1536]{0:T(1024)S(1)} %reshape.121, f32[1536,384]{0,1:T(8,128)} %fusion.18, f32[1536,384]{0,1:T(8,128)} %fusion.22), kind=kOutput, calls=%fused_computation.33 | convolution fusion | flops 2420047872 | bytes 14161920 | tf_op jit(solution)/shard_map/dot_general | solution.py:30
  432.1 8.4 %multiply_reduce_fusion = (bf16[1536]{0:T(1024)(128)(2,1)S(1)}, bf16[1536,384]{0,1:T(8,128)(2,1)S(1)}, bf16[1536,384]{0,1:T(8,128)(2,1)S(1)}) fusion(f32[1536,384]{0,1:T(8,128)} %fusion.18, f32[1536,384]{0,1:T(8,128)} %fusion.22, f32[1536]{0:T(1024)S(1)} %reshape.121, bf16[1536,2048]{1,0:T(8,128)(2,1)} %bitcast.8, bf16[2048,1152]{1,0:T(8,128)(2,1)} %bitcast.73), kind=kOutput, calls=%fused_computation.16 | convolution fusion | flops 2425944576 | bytes 14951424 | tf_op jit(solution)/shard_map/dot_general | solution.py:20
  440.5 5.2 fusion.56
  445.8 4.7 fusion.57
  454.1 4.9 fusion.20
  459.0 5.5 add_convert_fusion
  466.9 40.9 %all_to_all.25 = bf16[8,192,1024]{2,1,0:T(8,128)(2,1)S(1)} all-to-all(bf16[8,192,1024]{2,1,0:T(8,128)(2,1)S(1)} %bitcast.81), channel_id=1, replica_groups=mesh['dp'=4,'node'=2,'lz'=8,'ly'=4] {'node','ly'}, dimensions={0} | all-to-all | bytes 6291456 | tf_op jit(solution)/shard_map/all_to_all | solution.py:132
  513.0 41.8 %all_to_all.26 = bf16[8,193,1024]{2,1,0:T(8,128)(2,1)S(1)} all-to-all(bf16[8,193,1024]{2,1,0:T(8,128)(2,1)S(1)} %fusion.3), channel_id=1, replica_groups=mesh['dp'=4,'node'=2,'lz'=8,'ly'=4] {'node','ly'}, dimensions={0} | all-to-all | bytes 6324224 | tf_op jit(solution)/shard_map/all_to_all | solution.py:129
  561.0 4.9 pad_maximum_fusion.1
  566.0 32.6 %reduce-scatter.11.cloned.1.call-done = f32[1,128,1024]{2,1,0:T(8,128)} async-done(((f32[8,128,1024]{2,1,0:T(8,128)}), f32[1,128,1024]{2,1,0:T(8,128)}) %reduce-scatter.11.cloned.1.call-update) | async-done | bytes 524304 | tf_op jit(solution)/shard_map/reduce_scatter | solution.py:158
  602.1 55.4 %reduce-scatter.9.cloned.1.call-done = f32[1,129,1024]{2,1,0:T(8,128)} async-done(((f32[8,129,1024]{2,1,0:T(8,128)}), f32[1,129,1024]{2,1,0:T(8,128)}) %reduce-scatter.9.cloned.1.call-update) | async-done | bytes 528400 | tf_op jit(solution)/shard_map/reduce_scatter | solution.py:154
  (84 shorter events, 55.7 us)
Async XLA Ops:
  7.2 232.2 %all-gather.7.cloned.1.call-start = ((), (), s32[]{:S(2)}) async-start(), calls=%async_computation.14 | async-start | bytes 4718592 | tf_op jit(solution)/shard_map/all_gather | solution.py:65
  206.2 5.9 copy-start.5
  206.2 5.9 copy-start.6
  206.2 57.5 %all-to-all-start.2 = ((bf16[4,2,294912]{2,1,0:T(2,128)(2,1)}), bf16[4,2,294912]{2,1,0:T(2,128)(2,1)}, u32[]{:S(2)}, u32[]{:S(2)}) async-start(bf16[4,2,294912]{2,1,0:T(2,128)(2,1)} %reshape.135), calls=%async_computation.2 | async-start | bytes 9437184 | tf_op jit(solution)/shard_map/all_to_all | solution.py:11
  211.3 61.9 %all-gather.5.cloned.1.call-start = ((), (), s32[]{:S(2)}) async-start(), calls=%async_computation.13 | async-start | bytes 4718592 | tf_op jit(solution)/shard_map/all_gather | solution.py:66
  263.7 82.4 %all-to-all-start.1 = ((bf16[8,193,2048]{2,1,0:T(8,128)(2,1)}), bf16[8,193,2048]{2,1,0:T(8,128)(2,1)}, u32[]{:S(2)}, u32[]{:S(2)}) async-start(bf16[8,193,2048]{2,1,0:T(8,128)(2,1)} %fusion.1), calls=%async_computation.1 | async-start | bytes 13107200 | tf_op jit(solution)/shard_map/all_to_all | solution.py:111
  346.1 76.3 %all-to-all-start = ((bf16[8,192,2048]{2,1,0:T(8,128)(2,1)}), bf16[8,192,2048]{2,1,0:T(8,128)(2,1)}, u32[]{:S(2)}, u32[]{:S(2)}) async-start(bf16[8,192,2048]{2,1,0:T(8,128)(2,1)} %bitcast.70), calls=%async_computation | async-start | bytes 12582912 | tf_op jit(solution)/shard_map/all_to_all | solution.py:112
  351.1 209.9 %reduce-scatter.5.cloned.1.call-start = ((), (), s32[]{:S(2)}) async-start(), calls=%async_computation.9 | async-start | bytes 3932160 | tf_op jit(solution)/shard_map/reduce_scatter | solution.py:147
  366.9 4.2 copy-start
  370.4 4.7 copy-start.2
  431.8 129.2 %reduce-scatter.7.cloned.1.call-start = ((), (), s32[]{:S(2)}) async-start(), calls=%async_computation.10 | async-start | bytes 7864320 | tf_op jit(solution)/shard_map/reduce_scatter | solution.py:148
  440.5 5.3 copy-start.4
  453.6 145.0 %reduce-scatter.11.cloned.1.call-start = ((), (), s32[]{:S(2)}) async-start(), calls=%async_computation.12 | async-start | bytes 4718592 | tf_op jit(solution)/shard_map/reduce_scatter | solution.py:158
  510.7 2.0 copy-start.1
  510.7 146.8 %reduce-scatter.9.cloned.1.call-start = ((), (), s32[]{:S(2)}) async-start(), calls=%async_computation.11 | async-start | bytes 5013504 | tf_op jit(solution)/shard_map/reduce_scatter | solution.py:154
  566.0 33.7 %copy-start.3 = (f32[512,768]{0,1:T(8,128)S(1)}, f32[512,768]{0,1:T(8,128)}, u32[]{:S(2)}) copy-start(f32[512,768]{0,1:T(8,128)} %reduce-scatter.7.cloned.1.call-done) | copy-start | bytes 4718596
Sparse Core Ops, SparseCore 0:
  9.8 58.6 all-gather.6
  213.9 59.2 all-gather.4
  431.9 40.4 reduce-scatter.4
  474.8 66.2 reduce-scatter.6
  543.5 55.0 reduce-scatter.10
  601.0 56.4 reduce-scatter.8
